TPU v7x, 512 devices: a whole 4x8x8 slice. The times are simulated.
512 devices in a mesh: grp: 8 (over y_lo, core), own: 64 (over x, y_hi, z).
Axes of the slice: x: 4, y: 8 (y_hi: 2, y_lo: 4; y = y_hi * 4 + y_lo), z: 8, core: 2. Of those that a mesh axis runs over, the one named last changes fastest.
Arguments:
- activations: bfloat16 [65536, 1024], P(('grp', 'own'))
- out_grads: bfloat16 [65536, 1024], P(('grp', 'own')), may hold values from -0.01953125 to 0.01953125
- master: float32 [1024, 1024], P('own'), may hold values from -6 to 6
- moment: float32 [1024, 1024], P('own'), may hold values from 0.05 to 5
- left_root: bfloat16 [1024, 1024], P('own'), may hold values from -0.25 to 2.25, as said below
- right_root: bfloat16 [1024, 1024], P('own'), may hold values from -0.25 to 2.25, as said below
- stats_in: float32 [256, 16, 1024], P('own'), may hold values from -6 to 6
- tile_slot: int32 [128], replicated, may hold values from 0 to 255, as said below
Outputs:
- master_out: float32 [1024, 1024], P('own')
- moment_out: float32 [1024, 1024], P('own')
- stats_out: float32 [256, 16, 1024], P('own')
- weights: bfloat16 [1024, 1024], replicated
Inputs may be any that keep to these rules, and one draw needn't show every extreme that they name: `tile_slot`: distinct slot numbers; slot s belongs to owner s // 4; some owner holds 4 tiles. `left_root`: symmetric. `right_root`: symmetric.
All inputs are finite; a program needn't handle non-finite values.
Results may differ from a plain program's by a relative error of at most 0.005.
Values may be sent and summed in bfloat16 or wider, within the bound.
No kernel may reach another device: no remote copies, remote signals or barrier semaphores. Data moves between devices by JAX's collectives and lax.ppermute only.
A program may use at most 64 MiB of HBM per device.

v0:
```python
import jax
import jax.numpy as jnp
from jax import lax
from jax.sharding import Mesh
from jax.sharding import PartitionSpec as P

stat_decay = 0.9
moment_decay = 0.95
learn_rate = 0.3
adam_eps = 1e-08
norm_eps = 1e-06
GRP = ("yl", "c")
OWN = ("x", "yh", "z")
SUB_SIZES = (4, 2, 4, 2, 8)


def split3(value):
    hi = lax.reduce_precision(value, exponent_bits=8, mantissa_bits=7)
    rest = value - hi
    mid = lax.reduce_precision(rest, exponent_bits=8, mantissa_bits=7)
    lo = lax.reduce_precision(rest - mid, exponent_bits=8, mantissa_bits=7)
    return jnp.stack([hi, mid, lo])


def gather_own_rows(block):
    rows = block.shape[0]
    out = block
    for axis in ("yh", "x", "z"):
        out = lax.all_gather(out, axis, axis=0, tiled=True)
    out = out.reshape(SUB_SIZES[4], SUB_SIZES[2], SUB_SIZES[3], rows, block.shape[1])
    out = jnp.transpose(out, (1, 2, 0, 3, 4))
    return out.reshape(-1, block.shape[1])


def local(activations, out_grads, master, moment, left_root, right_root, stats_in, tile_slot):
    owner_rows = master.shape[0]
    block_size = master.shape[1]
    owners = block_size // owner_rows
    capacity = stats_in.shape[0]
    tile_rows = stats_in.shape[1]
    tile_count = tile_slot.shape[0]
    owner_index = lax.axis_index(OWN)
    grp_size = SUB_SIZES[0] * SUB_SIZES[1]
    right_full = gather_own_rows(right_root)
    partial = lax.dot_general(
        activations, out_grads, (((0,), (0,)), ((), ())), preferred_element_type=jnp.float32
    )
    pieces = lax.all_to_all(partial.reshape(owners, owner_rows, block_size), OWN, 0, 0, tiled=True)
    own_sum = jnp.sum(pieces, axis=0)
    copies = jnp.broadcast_to(own_sum[None], (grp_size, owner_rows, block_size))
    grad_rows = jnp.sum(lax.all_to_all(copies, GRP, 0, 0, tiled=True), axis=0)
    moment_out = moment_decay * moment + (1.0 - moment_decay) * grad_rows * grad_rows
    adam_dir = grad_rows / (jnp.sqrt(moment_out) + adam_eps)
    adam_part = split3(jnp.sum(adam_dir * adam_dir))
    extra = jnp.zeros((1, block_size), jnp.float32).at[0, :3].set(adam_part)
    payload = jnp.concatenate([grad_rows, extra], axis=0).astype(jnp.bfloat16)
    sent = jnp.broadcast_to(payload[None], (owners,) + payload.shape)
    got = lax.all_to_all(sent, OWN, 0, 0, tiled=True)
    grad_low = got[:, :owner_rows, :].reshape(block_size, block_size)
    adam_sum = jnp.sum(got[:, owner_rows, :3].astype(jnp.float32))
    left_mid = jnp.dot(left_root, grad_low, preferred_element_type=jnp.float32).astype(jnp.bfloat16)
    precond = jnp.dot(left_mid, right_full, preferred_element_type=jnp.float32)
    precond_part = jnp.broadcast_to(jnp.sum(precond * precond), (owners, 1, 128))
    precond_sum = jnp.sum(lax.all_to_all(precond_part, OWN, 0, 0, tiled=True)[:, 0, 0])
    graft_scale = jnp.sqrt(adam_sum) / (jnp.sqrt(precond_sum) + norm_eps)
    master_out = master - learn_rate * graft_scale * precond
    weight_rows = jnp.broadcast_to(
        master_out.astype(jnp.bfloat16)[None], (owners, owner_rows, block_size)
    )
    weights = lax.all_to_all(weight_rows, OWN, 0, 0, tiled=True).reshape(block_size, block_size)
    my_slots = owner_index * capacity + jnp.arange(capacity, dtype=jnp.int32)
    matches = (tile_slot[:, None] == my_slots[None, :]).astype(jnp.int32)
    tile_ids = jnp.sum(matches * jnp.arange(tile_count, dtype=jnp.int32)[:, None], axis=0)
    filled = jnp.sum(matches, axis=0)
    per_half = block_size // tile_rows
    which_half = tile_ids // per_half
    offsets = (tile_ids - which_half * per_half) * tile_rows
    grad_low_t = grad_low.T
    row_blocks = jnp.concatenate(
        [lax.dynamic_slice_in_dim(grad_low, offsets[s], tile_rows, 0) for s in range(capacity)],
        axis=0,
    )
    col_blocks = jnp.concatenate(
        [lax.dynamic_slice_in_dim(grad_low_t, offsets[s], tile_rows, 0) for s in range(capacity)],
        axis=0,
    )
    left_tiles = lax.dot_general(
        row_blocks, grad_low, (((1,), (1,)), ((), ())), preferred_element_type=jnp.float32
    ).reshape(capacity, tile_rows, block_size)
    right_tiles = jnp.dot(col_blocks, grad_low, preferred_element_type=jnp.float32).reshape(
        capacity, tile_rows, block_size
    )
    product = jnp.where((which_half == 0)[:, None, None], left_tiles, right_tiles)
    fresh = stat_decay * stats_in + (1.0 - stat_decay) / block_size * product
    stats_out = jnp.where((filled > 0)[:, None, None], fresh, 0.0)
    return (master_out, moment_out, stats_out, weights)


def solution(mesh):
    sub_mesh = Mesh(mesh.devices.reshape(SUB_SIZES), GRP + OWN)
    rows_all = P(GRP + OWN, None)
    rows_own = P(OWN, None)
    in_specs = (rows_all, rows_all, rows_own, rows_own, rows_own, rows_own, P(OWN, None, None), P())
    out_specs = (rows_own, rows_own, P(OWN, None, None), P())
    return jax.shard_map(
        local, mesh=sub_mesh, in_specs=in_specs, out_specs=out_specs, check_vma=False
    )
```

profile of v0, /device:TPU:8, one launch (start us, length us, event | category | flops | bytes accessed | tf_op | source)
XLA Modules:
  0.0 407.6 jit_solution(5947708179712578350)
XLA Ops:
  7.2 0.0 copy-start
  7.2 0.9 copy-done
  8.1 1.7 fusion.12
  9.8 122.6 %all_to_all.25 = f32[64,16,1024]{2,1,0:T(8,128)} all-to-all(f32[64,16,1024]{2,1,0:T(8,128)S(1)} %bitcast.42), channel_id=1, replica_groups=mesh['yl'=4,'c'=2,'x'=4,'yh'=2,'z'=8] {'x','yh','z'}, dimensions={0} | all-to-all | bytes 8388608 | tf_op jit(solution)/shard_map/all_to_all | solution.py:48
  132.4 2.4 reduce_sum.72
  134.8 0.0 copy-start.2
  134.8 0.8 broadcast_in_dim.24
  135.6 3.4 all-to-all-start.1
  139.1 0.6 compare_reduce_fusion
  139.7 11.3 %all-to-all-done.1 = f32[8,16,1024]{2,1,0:T(8,128)S(1)} async-done(((f32[8,16,1024]{2,1,0:T(8,128)}), f32[8,16,1024]{2,1,0:T(8,128)S(1)}, u32[]{:S(2)}, u32[]{:S(2)}) %all-to-all-start.1) | async-done | bytes 524320 | tf_op jit(solution)/shard_map/all_to_all | solution.py:51
  151.1 0.0 copy-done.2
  151.1 1.3 multiply_reduce_fusion.1
  156.5 2.7 fusion.8
  159.3 2.1 broadcast_in_dim.25
  161.4 6.8 %all-to-all-start.2 = ((bf16[64,17,1024]{2,1,0:T(8,128)(2,1)}), bf16[64,17,1024]{2,1,0:T(8,128)(2,1)}, u32[]{:S(2)}, u32[]{:S(2)}) async-start(bf16[64,17,1024]{2,1,0:T(8,128)(2,1)} %broadcast_in_dim.25), calls=%async_computation.2 | async-start | bytes 6291456 | tf_op jit(solution)/shard_map/all_to_all | solution.py:58
  168.2 0.0 all-gather.2.cloned.1.call-start
  168.3 0.0 copy-done.5
  168.3 53.6 %all_gather.9 = bf16[32,1024]{1,0:T(8,128)(2,1)S(1)} all-gather(bf16[16,1024]{1,0:T(8,128)(2,1)S(1)} %copy-done.5), channel_id=1, replica_groups=mesh['yl'=4,'c'=2,'x'=4,'yh'=2,'z'=8] {'yh'}, dimensions={0}, use_global_device_ids=true | all-gather | bytes 98304 | tf_op jit(solution)/shard_map/all_gather | solution.py:29
  221.9 19.4 %all_gather.10 = bf16[128,1024]{1,0:T(8,128)(2,1)} all-gather(bf16[32,1024]{1,0:T(8,128)(2,1)S(1)} %all_gather.9), channel_id=1, replica_groups=mesh['yl'=4,'c'=2,'x'=4,'yh'=2,'z'=8] {'x'}, dimensions={0}, use_global_device_ids=true | all-gather | bytes 327680 | tf_op jit(solution)/shard_map/all_gather | solution.py:29
  241.3 0.0 all-gather.2.cloned.1.call-update
  241.3 58.9 %all-gather.2.cloned.1.call-done = bf16[1024,1024]{1,0:T(8,128)(2,1)} async-done(((bf16[128,1024]{1,0:T(8,128)(2,1)}), bf16[1024,1024]{1,0:T(8,128)(2,1)}) %all-gather.2.cloned.1.call-update) | async-done | bytes 2097168 | tf_op jit(solution)/shard_map/all_gather | solution.py:29
  300.2 3.2 copy.18
  303.4 0.0 all-to-all-done.2
  303.4 1.9 slice.49
  305.3 0.0 copy-done.4
  305.3 0.0 copy-start.3
  305.3 2.9 multiply_reduce_fusion
  308.2 1.3 broadcast_in_dim.26
  309.5 11.8 %all-to-all-start.3 = ((f32[64,1,128]{2,1,0:T(1,128)}), f32[64,1,128]{2,1,0:T(1,128)S(1)}, u32[]{:S(2)}, u32[]{:S(2)}) async-start(f32[64,1,128]{2,1,0:T(1,128)} %broadcast_in_dim.26), calls=%async_computation.3 | async-start | bytes 65536 | tf_op jit(solution)/shard_map/all_to_all | solution.py:64
  321.3 1.6 fusion.5
  323.6 12.0 %all-to-all-done.3 = f32[64,1,128]{2,1,0:T(1,128)S(1)} async-done(((f32[64,1,128]{2,1,0:T(1,128)}), f32[64,1,128]{2,1,0:T(1,128)S(1)}, u32[]{:S(2)}, u32[]{:S(2)}) %all-to-all-start.3) | async-done | bytes 32800 | tf_op jit(solution)/shard_map/all_to_all | solution.py:64
  335.5 0.7 slice_reduce_fusion
  336.9 0.0 copy-done.3
  337.0 0.6 fusion.9
  337.6 1.6 broadcast_in_dim.53
  339.2 5.7 %all-to-all-start.4 = ((bf16[64,16,1024]{2,1,0:T(8,128)(2,1)}), bf16[64,16,1024]{2,1,0:T(8,128)(2,1)}, u32[]{:S(2)}, u32[]{:S(2)}) async-start(bf16[64,16,1024]{2,1,0:T(8,128)(2,1)} %broadcast_in_dim.53), calls=%async_computation.4 | async-start | bytes 4194304 | tf_op jit(solution)/shard_map/all_to_all | solution.py:70
  344.9 0.0 copy-done.6
  344.9 0.2 fusion.6
  345.1 0.6 fusion.11
  353.2 0.4 dynamic-slice_bitcast_fusion.3
  353.7 0.0 copy-start.1
  353.7 0.4 pad_maximum_fusion
  354.0 0.1 copy.20
  354.2 0.1 constant_dynamic-slice_fusion.3
  354.2 0.8 fusion.13
  355.0 1.2 fusion.2
  356.2 41.4 %all-to-all-done.4 = bf16[64,16,1024]{2,1,0:T(8,128)(2,1)} async-done(((bf16[64,16,1024]{2,1,0:T(8,128)(2,1)}), bf16[64,16,1024]{2,1,0:T(8,128)(2,1)}, u32[]{:S(2)}, u32[]{:S(2)}) %all-to-all-start.4) | async-done | bytes 2097184 | tf_op jit(solution)/shard_map/all_to_all | solution.py:70
  397.7 3.1 copy.23
  (12 shorter events, 0.1 us)
Async XLA Ops:
  7.2 1.0 copy-start
  134.8 16.3 %copy-start.2 = (f32[16,1024]{1,0:T(8,128)S(1)}, f32[16,1024]{1,0:T(8,128)}, u32[]{:S(2)}) copy-start(f32[16,1024]{1,0:T(8,128)} %param.13) | copy-start | bytes 196612
  135.6 15.4 %all-to-all-start.1 = ((f32[8,16,1024]{2,1,0:T(8,128)}), f32[8,16,1024]{2,1,0:T(8,128)S(1)}, u32[]{:S(2)}, u32[]{:S(2)}) async-start(f32[8,16,1024]{2,1,0:T(8,128)} %broadcast_in_dim.24), calls=%async_computation.1 | async-start | bytes 1048576 | tf_op jit(solution)/shard_map/all_to_all | solution.py:51
  161.4 6.9 %copy-start.5 = (bf16[16,1024]{1,0:T(8,128)(2,1)S(1)}, bf16[16,1024]{1,0:T(8,128)(2,1)}, u32[]{:S(2)}) copy-start(bf16[16,1024]{1,0:T(8,128)(2,1)} %param.15) | copy-start | bytes 98308
  161.4 142.0 %all-to-all-start.2 = ((bf16[64,17,1024]{2,1,0:T(8,128)(2,1)}), bf16[64,17,1024]{2,1,0:T(8,128)(2,1)}, u32[]{:S(2)}, u32[]{:S(2)}) async-start(bf16[64,17,1024]{2,1,0:T(8,128)(2,1)} %broadcast_in_dim.25), calls=%async_computation.2 | async-start | bytes 6291456 | tf_op jit(solution)/shard_map/all_to_all | solution.py:58
  168.2 132.0 %all-gather.2.cloned.1.call-start = ((), (), s32[]{:S(2)}) async-start(), calls=%async_computation.5 | async-start | bytes 2359296 | tf_op jit(solution)/shard_map/all_gather | solution.py:29
  303.4 1.9 copy-start.4
  305.3 31.6 %copy-start.3 = (f32[16,1024]{1,0:T(8,128)S(1)}, f32[16,1024]{1,0:T(8,128)}, u32[]{:S(2)}) copy-start(f32[16,1024]{1,0:T(8,128)} %param.12) | copy-start | bytes 196612
  309.5 26.0 %all-to-all-start.3 = ((f32[64,1,128]{2,1,0:T(1,128)}), f32[64,1,128]{2,1,0:T(1,128)S(1)}, u32[]{:S(2)}, u32[]{:S(2)}) async-start(f32[64,1,128]{2,1,0:T(1,128)} %broadcast_in_dim.26), calls=%async_computation.3 | async-start | bytes 65536 | tf_op jit(solution)/shard_map/all_to_all | solution.py:64
  339.2 5.7 %copy-start.6 = (s32[128]{0:T(128)S(1)}, s32[128]{0:T(128)}, u32[]{:S(2)}) copy-start(s32[128]{0:T(128)} %param.17) | copy-start | bytes 1540
  339.2 58.5 %all-to-all-start.4 = ((bf16[64,16,1024]{2,1,0:T(8,128)(2,1)}), bf16[64,16,1024]{2,1,0:T(8,128)(2,1)}, u32[]{:S(2)}, u32[]{:S(2)}) async-start(bf16[64,16,1024]{2,1,0:T(8,128)(2,1)} %broadcast_in_dim.53), calls=%async_computation.4 | async-start | bytes 4194304 | tf_op jit(solution)/shard_map/all_to_all | solution.py:70
  353.7 1.3 copy-start.1
Sparse Core Ops, SparseCore 0:
  241.4 58.7 all-gather.1
where the time goes:
time: 409 us; the launch traced here: 408 us
  blocking collectives  196 us (48%)
  waiting for transfers between devices  124 us (30%)
  starting transfers between devices  27.8 us (7%)
  between operations  27.3 us (7%)
  local copies, waits for them, and re-layouts  16.2 us (4%)
  other arithmetic  10.5 us (3%)
  matrix products  6.56 us (2%)
    all_to_all x1, blocking collectives, local(): lax.all_to_all(partial.reshape(owners, owner_rows, block_size), OWN, 0, 0...  123 us
    all_gather x2, blocking collectives, gather_own_rows(): out = lax.all_gather(out, axis, axis=0, tiled=True)  73 us
    all_gather x1, waiting for transfers between devices, gather_own_rows(): out = lax.all_gather(out, axis, axis=0, tiled=True)  58.9 us
    all_to_all x1, waiting for transfers between devices, local(): lax.all_to_all(weight_rows, OWN, 0, 0, tiled=True)  41.4 us
    all_to_all x1, waiting for transfers between devices, local(): lax.all_to_all(precond_part, OWN, 0, 0, tiled=True)[:, 0, 0]  12 us
    all_to_all x1, starting transfers between devices, local(): lax.all_to_all(precond_part, OWN, 0, 0, tiled=True)[:, 0, 0]  11.8 us
    all_to_all x1, waiting for transfers between devices, local(): grad_rows = jnp.sum(lax.all_to_all(copies, GRP, 0, 0, tiled=True), axis=0)  11.3 us
  transfers between devices with their start and end apart: 5, of which 4 were waited for; matrix products, arithmetic and copies ran while one was open for 2% of the time, Pallas kernels for 0%

commit v1 on v0

--- a/solution.py
+++ b/solution.py
@@ -26,7 +26,9 @@
     rows = block.shape[0]
     out = block
     for axis in ("yh", "x", "z"):
-        out = lax.all_gather(out, axis, axis=0, tiled=True)
+        out = jnp.concatenate(
+            lax.all_to_all(jnp.stack([out] * lax.axis_size(axis)), axis, 0, 0), axis=0
+        )
     out = out.reshape(SUB_SIZES[4], SUB_SIZES[2], SUB_SIZES[3], rows, block.shape[1])
     out = jnp.transpose(out, (1, 2, 0, 3, 4))
     return out.reshape(-1, block.shape[1])

time: 409 us -> 399 us (0.976)
  the two profiles are of different devices: /device:TPU:8 before, /device:TPU:2 now
where the time goes in v1:
time: 399 us; the launch traced here: 398 us
  waiting for transfers between devices  175 us (44%)
  blocking collectives  135 us (34%)
  starting transfers between devices  38.8 us (10%)
  local copies, waits for them, and re-layouts  15.2 us (4%)
  between operations  13.9 us (3%)
  other arithmetic  11.9 us (3%)
  matrix products  8.48 us (2%)
    all_to_all x1, blocking collectives, local(): lax.all_to_all(partial.reshape(owners, owner_rows, block_size), OWN, 0, 0...  114 us
    all_to_all x1, waiting for transfers between devices, local(): got = lax.all_to_all(sent, OWN, 0, 0, tiled=True)  74.6 us
    all_to_all x3, waiting for transfers between devices, gather_own_rows(): lax.all_to_all(jnp.stack([out] * lax.axis_size(axis)), axis, 0, 0)  49.5 us
    all_to_all x1, waiting for transfers between devices, local(): lax.all_to_all(weight_rows, OWN, 0, 0, tiled=True)  39.7 us
    all_to_all x1, blocking collectives, local(): grad_rows = jnp.sum(lax.all_to_all(copies, GRP, 0, 0, tiled=True), axis=0)  20.6 us
    all_to_all x3, starting transfers between devices, gather_own_rows(): lax.all_to_all(jnp.stack([out] * lax.axis_size(axis)), axis, 0, 0)  15.6 us
    all_to_all x1, waiting for transfers between devices, local(): lax.all_to_all(precond_part, OWN, 0, 0, tiled=True)[:, 0, 0]  11 us
    all_to_all x1, starting transfers between devices, local(): lax.all_to_all(precond_part, OWN, 0, 0, tiled=True)[:, 0, 0]  10.2 us
  transfers between devices with their start and end apart: 6, of which 6 were waited for; matrix products, arithmetic and copies ran while one was open for 4% of the time, Pallas kernels for 0%

profile of v1, /device:TPU:2, one launch (start us, length us, event | category | flops | bytes accessed | tf_op | source)
XLA Modules:
  0.0 398.2 jit_solution(1630914862766963918)
XLA Ops:
  0.6 0.0 copy-start
  0.6 1.5 pad_maximum_fusion.2
  2.1 7.1 %all-to-all-start.3 = ((bf16[2,16,1024]{2,1,0:T(8,128)(2,1)}), bf16[2,16,1024]{2,1,0:T(8,128)(2,1)S(1)}, u32[]{:S(2)}, u32[]{:S(2)}) async-start(bf16[2,16,1024]{2,1,0:T(8,128)(2,1)} %pad_maximum_fusion.2), calls=%async_computation.3 | async-start | bytes 131072 | tf_op jit(solution)/shard_map/all_to_all | solution.py:30
  9.2 0.0 copy-done
  9.2 3.6 fusion.12
  12.8 4.4 %all-to-all-done.3 = bf16[2,16,1024]{2,1,0:T(8,128)(2,1)S(1)} async-done(((bf16[2,16,1024]{2,1,0:T(8,128)(2,1)}), bf16[2,16,1024]{2,1,0:T(8,128)(2,1)S(1)}, u32[]{:S(2)}, u32[]{:S(2)}) %all-to-all-start.3) | async-done | bytes 65568 | tf_op jit(solution)/shard_map/all_to_all | solution.py:30
  17.2 114.4 %all_to_all.40 = f32[64,16,1024]{2,1,0:T(8,128)} all-to-all(f32[64,16,1024]{2,1,0:T(8,128)} %bitcast.45), channel_id=1, replica_groups=mesh['yl'=4,'c'=2,'x'=4,'yh'=2,'z'=8] {'x','yh','z'}, dimensions={0} | all-to-all | bytes 8388608 | tf_op jit(solution)/shard_map/all_to_all | solution.py:50
  131.7 0.7 stack.31
  132.4 4.7 %all-to-all-start.4 = ((bf16[4,32,1024]{2,1,0:T(8,128)(2,1)}), bf16[4,32,1024]{2,1,0:T(8,128)(2,1)S(1)}, u32[]{:S(2)}, u32[]{:S(2)}) async-start(bf16[4,32,1024]{2,1,0:T(8,128)(2,1)} %stack.31), calls=%async_computation.4 | async-start | bytes 524288 | tf_op jit(solution)/shard_map/all_to_all | solution.py:30
  137.1 2.4 reduce_sum.72
  139.5 2.8 all-to-all-done.4
  142.4 20.6 %all_to_all.41 = f32[8,16,1024]{2,1,0:T(8,128)S(1)} all-to-all(f32[8,16,1024]{2,1,0:T(8,128)S(1)} %broadcast_in_dim.24), channel_id=1, replica_groups=mesh['yl'=4,'c'=2,'x'=4,'yh'=2,'z'=8] {'yl','c'}, dimensions={0} | all-to-all | bytes 1048576 | tf_op jit(solution)/shard_map/all_to_all | solution.py:53
  163.0 1.6 stack.32
  164.6 3.7 all-to-all-start.5
  168.4 0.6 compare_reduce_fusion
  169.0 0.0 copy-done.2
  169.0 1.3 multiply_reduce_fusion.1
  174.5 2.6 fusion.8
  177.2 42.2 %all-to-all-done.5 = bf16[8,128,1024]{2,1,0:T(8,128)(2,1)S(1)} async-done(((bf16[8,128,1024]{2,1,0:T(8,128)(2,1)}), bf16[8,128,1024]{2,1,0:T(8,128)(2,1)S(1)}, u32[]{:S(2)}, u32[]{:S(2)}) %all-to-all-start.5) | async-done | bytes 2097184 | tf_op jit(solution)/shard_map/all_to_all | solution.py:30
  219.4 2.1 broadcast_in_dim.25
  221.5 6.5 %all-to-all-start.2 = ((bf16[64,17,1024]{2,1,0:T(8,128)(2,1)}), bf16[64,17,1024]{2,1,0:T(8,128)(2,1)}, u32[]{:S(2)}, u32[]{:S(2)}) async-start(bf16[64,17,1024]{2,1,0:T(8,128)(2,1)} %broadcast_in_dim.25), calls=%async_computation.2 | async-start | bytes 6291456 | tf_op jit(solution)/shard_map/all_to_all | solution.py:60
  228.0 1.6 copy.18
  229.6 74.6 %all-to-all-done.2 = bf16[64,17,1024]{2,1,0:T(8,128)(2,1)} async-done(((bf16[64,17,1024]{2,1,0:T(8,128)(2,1)}), bf16[64,17,1024]{2,1,0:T(8,128)(2,1)}, u32[]{:S(2)}, u32[]{:S(2)}) %all-to-all-start.2) | async-done | bytes 2228256 | tf_op jit(solution)/shard_map/all_to_all | solution.py:60
  304.3 1.9 slice.49
  306.2 0.0 copy-done.4
  306.2 0.0 copy-start.3
  306.2 2.9 multiply_reduce_fusion
  309.1 1.3 broadcast_in_dim.26
  310.4 10.2 %all-to-all-start.6 = ((f32[64,1,128]{2,1,0:T(1,128)}), f32[64,1,128]{2,1,0:T(1,128)S(1)}, u32[]{:S(2)}, u32[]{:S(2)}) async-start(f32[64,1,128]{2,1,0:T(1,128)} %broadcast_in_dim.26), calls=%async_computation.6 | async-start | bytes 65536 | tf_op jit(solution)/shard_map/all_to_all | solution.py:66
  320.6 1.6 fusion.5
  322.8 11.0 %all-to-all-done.6 = f32[64,1,128]{2,1,0:T(1,128)S(1)} async-done(((f32[64,1,128]{2,1,0:T(1,128)}), f32[64,1,128]{2,1,0:T(1,128)S(1)}, u32[]{:S(2)}, u32[]{:S(2)}) %all-to-all-start.6) | async-done | bytes 32800 | tf_op jit(solution)/shard_map/all_to_all | solution.py:66
  333.8 0.7 slice_reduce_fusion
  335.2 0.0 copy-done.3
  335.3 0.6 fusion.9
  335.9 1.6 broadcast_in_dim.53
  337.5 6.6 %all-to-all-start.7 = ((bf16[64,16,1024]{2,1,0:T(8,128)(2,1)}), bf16[64,16,1024]{2,1,0:T(8,128)(2,1)}, u32[]{:S(2)}, u32[]{:S(2)}) async-start(bf16[64,16,1024]{2,1,0:T(8,128)(2,1)} %broadcast_in_dim.53), calls=%async_computation.7 | async-start | bytes 4194304 | tf_op jit(solution)/shard_map/all_to_all | solution.py:72
  344.1 0.2 fusion.6
  344.3 0.6 fusion.11
  352.4 0.5 dynamic-slice_bitcast_fusion.3
  352.9 0.0 copy-start.1
  352.9 0.4 pad_maximum_fusion
  353.2 0.1 copy.20
  353.4 0.1 constant_dynamic-slice_fusion.3
  353.4 0.8 fusion.13
  354.2 0.0 copy-done.1
  354.2 1.2 fusion.2
  355.4 39.7 %all-to-all-done.7 = bf16[64,16,1024]{2,1,0:T(8,128)(2,1)} async-done(((bf16[64,16,1024]{2,1,0:T(8,128)(2,1)}), bf16[64,16,1024]{2,1,0:T(8,128)(2,1)}, u32[]{:S(2)}, u32[]{:S(2)}) %all-to-all-start.7) | async-done | bytes 2097184 | tf_op jit(solution)/shard_map/all_to_all | solution.py:72
  395.1 3.1 copy.23
  (13 shorter events, 0.1 us)
Async XLA Ops:
  0.6 8.6 %copy-start = (bf16[128,1024]{1,0:T(8,128)(2,1)S(1)}, bf16[128,1024]{1,0:T(8,128)(2,1)}, u32[]{:S(2)}) copy-start(bf16[128,1024]{1,0:T(8,128)(2,1)} %param.10) | copy-start | bytes 786436
  2.1 15.1 %all-to-all-start.3 = ((bf16[2,16,1024]{2,1,0:T(8,128)(2,1)}), bf16[2,16,1024]{2,1,0:T(8,128)(2,1)S(1)}, u32[]{:S(2)}, u32[]{:S(2)}) async-start(bf16[2,16,1024]{2,1,0:T(8,128)(2,1)} %pad_maximum_fusion.2), calls=%async_computation.3 | async-start | bytes 131072 | tf_op jit(solution)/shard_map/all_to_all | solution.py:30
  132.4 10.0 %all-to-all-start.4 = ((bf16[4,32,1024]{2,1,0:T(8,128)(2,1)}), bf16[4,32,1024]{2,1,0:T(8,128)(2,1)S(1)}, u32[]{:S(2)}, u32[]{:S(2)}) async-start(bf16[4,32,1024]{2,1,0:T(8,128)(2,1)} %stack.31), calls=%async_computation.4 | async-start | bytes 524288 | tf_op jit(solution)/shard_map/all_to_all | solution.py:30
  164.6 4.4 %copy-start.2 = (f32[16,1024]{1,0:T(8,128)S(1)}, f32[16,1024]{1,0:T(8,128)}, u32[]{:S(2)}) copy-start(f32[16,1024]{1,0:T(8,128)} %param.13) | copy-start | bytes 196612
  164.6 54.8 %all-to-all-start.5 = ((bf16[8,128,1024]{2,1,0:T(8,128)(2,1)}), bf16[8,128,1024]{2,1,0:T(8,128)(2,1)S(1)}, u32[]{:S(2)}, u32[]{:S(2)}) async-start(bf16[8,128,1024]{2,1,0:T(8,128)(2,1)} %stack.32), calls=%async_computation.5 | async-start | bytes 4194304 | tf_op jit(solution)/shard_map/all_to_all | solution.py:30
  221.5 82.8 %all-to-all-start.2 = ((bf16[64,17,1024]{2,1,0:T(8,128)(2,1)}), bf16[64,17,1024]{2,1,0:T(8,128)(2,1)}, u32[]{:S(2)}, u32[]{:S(2)}) async-start(bf16[64,17,1024]{2,1,0:T(8,128)(2,1)} %broadcast_in_dim.25), calls=%async_computation.2 | async-start | bytes 6291456 | tf_op jit(solution)/shard_map/all_to_all | solution.py:60
  229.6 76.5 %copy-start.4 = (bf16[16,1024]{1,0:T(8,128)(2,1)S(1)}, bf16[16,1024]{1,0:T(8,128)(2,1)}, u32[]{:S(2)}) copy-start(bf16[16,1024]{1,0:T(8,128)(2,1)} %param.14) | copy-start | bytes 98308
  306.2 29.1 %copy-start.3 = (f32[16,1024]{1,0:T(8,128)S(1)}, f32[16,1024]{1,0:T(8,128)}, u32[]{:S(2)}) copy-start(f32[16,1024]{1,0:T(8,128)} %param.12) | copy-start | bytes 196612
  310.4 23.5 %all-to-all-start.6 = ((f32[64,1,128]{2,1,0:T(1,128)}), f32[64,1,128]{2,1,0:T(1,128)S(1)}, u32[]{:S(2)}, u32[]{:S(2)}) async-start(f32[64,1,128]{2,1,0:T(1,128)} %broadcast_in_dim.26), calls=%async_computation.6 | async-start | bytes 65536 | tf_op jit(solution)/shard_map/all_to_all | solution.py:66
  337.5 6.6 %copy-start.5 = (s32[128]{0:T(128)S(1)}, s32[128]{0:T(128)}, u32[]{:S(2)}) copy-start(s32[128]{0:T(128)} %param.17) | copy-start | bytes 1540
  337.5 57.7 %all-to-all-start.7 = ((bf16[64,16,1024]{2,1,0:T(8,128)(2,1)}), bf16[64,16,1024]{2,1,0:T(8,128)(2,1)}, u32[]{:S(2)}, u32[]{:S(2)}) async-start(bf16[64,16,1024]{2,1,0:T(8,128)(2,1)} %broadcast_in_dim.53), calls=%async_computation.7 | async-start | bytes 4194304 | tf_op jit(solution)/shard_map/all_to_all | solution.py:72
  352.9 1.3 copy-start.1
